TPU v7x, 256 devices: a whole 4x4x8 slice. The times are simulated.
256 devices in a mesh: gx: 64 (over x, y, z_hi, core), gy: 4 (over z_lo).
Axes of the slice: x: 4, y: 4, z: 8 (z_hi: 2, z_lo: 4; z = z_hi * 4 + z_lo), core: 2. Of those that a mesh axis runs over, the one named last changes fastest.
Arguments:
- features: bfloat16 [64, 4, 2, 8, 8, 8, 128], P('gx', 'gy'), may hold values from -6 to 6
- cotangent: bfloat16 [64, 4, 2, 4, 4, 4, 256], P('gx', 'gy'), may hold values from -6 to 6
- conv_first: bfloat16 [27, 128, 128], replicated, may hold values from -0.109375 to 0.109375
- down_weight: bfloat16 [8, 128, 256], replicated, may hold values from -0.1875 to 0.1875
- conv_second: bfloat16 [27, 256, 256], replicated, may hold values from -0.078125 to 0.078125
- block_count: int32 [64, 4], P('gx', 'gy'), may hold values from 1 to 2, as said below
- neighbours: int32 [64, 4, 2, 26], P('gx', 'gy'), may hold values from -1 to 1, as said below
Outputs:
- output_field: bfloat16 [64, 4, 2, 4, 4, 4, 256], P('gx', 'gy')
- input_grad: bfloat16 [64, 4, 2, 8, 8, 8, 128], P('gx', 'gy')
- grad_first: float32 [27, 128, 128], P(None, 'gx')
- grad_down: float32 [8, 128, 256], P(None, 'gx')
- grad_second: float32 [27, 256, 256], P(None, 'gx')
Inputs may be any that keep to these rules, and one draw needn't show every extreme that they name: `block_count`: each column holds 1 to 2 active blocks at distinct levels of its 8, in slots 0 up to its count in rising level; some column holds exactly 2. neighbours[i, j, s, k] is the slot, in column (i + ox, j + oy), of the active block oz levels from slot s's block, for the k-th nonzero offset (ox, oy, oz) with ox slowest and oz fastest, or -1 where there is none; it is below that column's count; rows of slots at or past block_count[i, j] are all -1; the relation is symmetric.
All inputs are finite; a program needn't handle non-finite values.
Results may differ from a plain program's by a relative error of at most 0.01.
Values may be sent and summed in bfloat16 or wider, within the bound.
No kernel may reach another device: no remote copies, remote signals or barrier semaphores. Data moves between devices by JAX's collectives and lax.ppermute only.
A program may use at most 128 MiB of HBM per device.

v0:
```python
import math

import jax
import jax.numpy as jnp
from jax import lax
from jax.sharding import PartitionSpec as P

NEIGHBOUR_STEPS = (-1, 0, 1)


def as_sent(shard):
    return jax.tree.map(lambda a: a.astype(jnp.bfloat16) if a.dtype == jnp.float32 else a, shard)


def shifted(block, axis, distance):
    devices = range(lax.axis_size(axis))
    route = [(i - distance, i) for i in devices if i - distance in devices]
    return lax.ppermute(block, axis, route)


def column_of(offset_x, offset_y, offset_z):
    raster = 9 * (offset_x + 1) + 3 * (offset_y + 1) + (offset_z + 1)
    return raster - 1 if raster > 13 else raster


def outer_layer(values, axis, border):
    length = values.shape[axis]
    first_index = 0 if border == 0 else length - 1
    return lax.slice_in_dim(values, first_index, first_index + 1, axis=axis)


def share_faces(fields):
    nearby = [dict() for member in fields]
    onward = [dict() for member in fields]
    for stride in (1, -1):
        border = 1 if stride == 1 else 0
        payload = []
        for volume in fields:
            planar = outer_layer(volume, 1, border)
            payload += [planar, outer_layer(planar, 2, 0), outer_layer(planar, 2, 1)]
        arrived = shifted(as_sent(tuple(payload)), "gx", stride)
        member = 0
        nearby[member][-stride, 0] = arrived[3 * member]
        onward[member][-stride, 0] = arrived[3 * member + 1]
        onward[member][-stride, 1] = arrived[3 * member + 2]
    for stride in (1, -1):
        border = 1 if stride == 1 else 0
        payload = []
        member = 0
        payload += [
            outer_layer(fields[member], 2, border),
            onward[member][-1, border],
            onward[member][1, border],
        ]
        arrived = shifted(as_sent(tuple(payload)), "gy", stride)
        member = 0
        nearby[member][0, -stride] = arrived[3 * member]
        nearby[member][-1, -stride] = arrived[3 * member + 1]
        nearby[member][1, -stride] = arrived[3 * member + 2]
    return nearby


def surround(center, nearby, slot_table):
    depth = center.shape[3]
    slabs_x = []
    for offset_x in NEIGHBOUR_STEPS:
        slabs_y = []
        for offset_y in NEIGHBOUR_STEPS:
            source = center if offset_x == 0 and offset_y == 0 else nearby[offset_x, offset_y]
            pieces = []
            for offset_z in NEIGHBOUR_STEPS:
                if offset_x == 0 and offset_y == 0 and (offset_z == 0):
                    pieces.append(center)
                else:
                    slot_ids = slot_table[:, column_of(offset_x, offset_y, offset_z)]
                    picked = jnp.take(source, jnp.maximum(slot_ids, 0), axis=0)
                    picked = jnp.where(
                        (slot_ids >= 0)[:, None, None, None, None],
                        picked,
                        jnp.zeros((), picked.dtype),
                    )
                    if offset_z == -1:
                        picked = picked[:, :, :, depth - 1 :]
                    elif offset_z == 1:
                        picked = picked[:, :, :, :1]
                    pieces.append(picked)
            slabs_y.append(jnp.concatenate(pieces, axis=3))
        slabs_x.append(jnp.concatenate(slabs_y, axis=2))
    return jnp.concatenate(slabs_x, axis=1)


def unfold(padded, extent):
    windows = []
    for along_x in range(3):
        for along_y in range(3):
            for along_z in range(3):
                windows.append(
                    padded[
                        :,
                        along_x : along_x + extent,
                        along_y : along_y + extent,
                        along_z : along_z + extent,
                        :,
                    ]
                )
    stacked = jnp.concatenate(windows, axis=-1)
    return stacked.reshape(-1, stacked.shape[-1])


def into_cells(blocks, half_edge):
    slot_count, channels = (blocks.shape[0], blocks.shape[-1])
    lattice = blocks.reshape(slot_count, half_edge, 2, half_edge, 2, half_edge, 2, channels)
    lattice = lattice.transpose(0, 1, 3, 5, 2, 4, 6, 7)
    return lattice.reshape(slot_count * half_edge**3, 8 * channels)


def from_cells(cell_rows, slot_count, half_edge, channels):
    lattice = cell_rows.reshape(slot_count, half_edge, half_edge, half_edge, 2, 2, 2, channels)
    lattice = lattice.transpose(0, 1, 4, 2, 5, 3, 6, 7)
    return lattice.reshape(slot_count, 2 * half_edge, 2 * half_edge, 2 * half_edge, channels)


def silu_slope(values):
    logistic = jax.nn.sigmoid(values)
    return logistic * (1.0 + values * (1.0 - logistic))


def contract_rows(left, right):
    return lax.dot_general(
        left, right, (((0,), (0,)), ((), ())), preferred_element_type=jnp.float32
    )


def body(features, cotangent, conv_first, down_weight, conv_second, block_count, neighbours):
    inputs = features[0, 0]
    slot_count, extent, channels = (inputs.shape[0], inputs.shape[1], inputs.shape[-1])
    half_edge = extent // 2
    wide_channels = conv_second.shape[-1]
    slot_table = neighbours[0, 0]
    live_mask = (jnp.arange(slot_count) < block_count[0, 0])[:, None, None, None, None]
    inputs = jnp.where(live_mask, inputs, jnp.zeros((), inputs.dtype))
    seed_blocks = jnp.where(live_mask, cotangent[0, 0], jnp.zeros((), inputs.dtype))
    near_input = share_faces((inputs,))[0]
    first_matrix = conv_first.reshape(-1, channels)
    first_cols = unfold(surround(inputs, near_input, slot_table), extent)
    pre_first = jnp.dot(first_cols, first_matrix, preferred_element_type=jnp.float32)
    hidden_first = jax.nn.silu(pre_first).astype(jnp.bfloat16)
    first_cells = into_cells(
        hidden_first.reshape(slot_count, extent, extent, extent, channels), half_edge
    )
    down_matrix = down_weight.reshape(-1, wide_channels)
    pre_down = jnp.dot(first_cells, down_matrix, preferred_element_type=jnp.float32)
    hidden_down = (
        jax.nn.silu(pre_down)
        .astype(jnp.bfloat16)
        .reshape(slot_count, half_edge, half_edge, half_edge, wide_channels)
    )
    near_hidden = share_faces((hidden_down,))[0]
    second_cols = unfold(surround(hidden_down, near_hidden, slot_table), half_edge)
    second_matrix = conv_second.reshape(-1, wide_channels)
    output_field = jnp.dot(second_cols, second_matrix, preferred_element_type=jnp.float32).astype(
        jnp.bfloat16
    )
    near_seed = share_faces((seed_blocks,))[0]
    seed_cols = unfold(surround(seed_blocks, near_seed, slot_table), half_edge)
    second_flip = jnp.transpose(conv_second[::-1], (0, 2, 1)).reshape(-1, wide_channels)
    back_down = jnp.dot(seed_cols, second_flip, preferred_element_type=jnp.float32)
    delta_down = (back_down * silu_slope(pre_down)).astype(jnp.bfloat16)
    grad_second = contract_rows(second_cols, seed_blocks.reshape(-1, wide_channels))
    grad_down = contract_rows(first_cells, delta_down)
    back_cells = lax.dot_general(
        delta_down, down_matrix, (((1,), (1,)), ((), ())), preferred_element_type=jnp.float32
    )
    back_first = from_cells(back_cells, slot_count, half_edge, channels).reshape(-1, channels)
    delta_first = (back_first * silu_slope(pre_first)).astype(jnp.bfloat16)
    delta_blocks = delta_first.reshape(slot_count, extent, extent, extent, channels)
    near_delta = share_faces((delta_blocks,))[0]
    delta_cols = unfold(surround(delta_blocks, near_delta, slot_table), extent)
    first_flip = jnp.transpose(conv_first[::-1], (0, 2, 1)).reshape(-1, channels)
    input_grad = jnp.dot(delta_cols, first_flip, preferred_element_type=jnp.float32).astype(
        jnp.bfloat16
    )
    grad_first = contract_rows(first_cols, delta_first)
    first_term = grad_first.reshape(27, channels, channels)
    down_term = grad_down.reshape(8, channels, wide_channels)
    second_term = grad_second.reshape(27, wide_channels, wide_channels)
    columns = (
        lax.psum_scatter(first_term, "gx", scatter_dimension=1, tiled=True),
        lax.psum_scatter(down_term, "gx", scatter_dimension=1, tiled=True),
        lax.psum_scatter(second_term, "gx", scatter_dimension=1, tiled=True),
    )
    summed = (
        lax.psum(columns[0].astype(jnp.bfloat16), "gy").astype(jnp.float32),
        lax.psum(columns[1].astype(jnp.bfloat16), "gy").astype(jnp.float32),
        lax.psum(columns[2].astype(jnp.bfloat16), "gy").astype(jnp.float32),
    )
    devices = lax.axis_size("gx") * lax.axis_size("gy")
    scale_first = 1.0 / math.sqrt(float(devices * slot_count * extent**3))
    scale_half = 1.0 / math.sqrt(float(devices * slot_count * half_edge**3))
    return (
        output_field.reshape(1, 1, slot_count, half_edge, half_edge, half_edge, wide_channels),
        input_grad.reshape(1, 1, slot_count, extent, extent, extent, channels),
        summed[0] * scale_first,
        summed[1] * scale_half,
        summed[2] * scale_half,
    )


def solution(mesh):
    placed = (
        P("gx", "gy", None, None, None, None, None),
        P("gx", "gy", None, None, None, None, None),
        P(),
        P(),
        P(),
        P("gx", "gy"),
        P("gx", "gy", None, None),
    )
    return jax.shard_map(
        body,
        mesh=mesh,
        in_specs=placed,
        out_specs=(
            P("gx", "gy", None, None, None, None, None),
            P("gx", "gy", None, None, None, None, None),
            P(None, "gx", None),
            P(None, "gx", None),
            P(None, "gx", None),
        ),
        check_vma=False,
    )
```

profile of v0, /device:TPU:2, one launch (start us, length us, event | category | flops | bytes accessed | tf_op | source)
XLA Modules:
  0.0 1120.0 jit_solution(13349509447897729206)
XLA Ops:
  9.0 1.9 collective-permute-start.3
  10.9 9.2 collective-permute-start
  20.1 3.7 collective-permute-start.7
  23.8 2.6 collective-permute-start.10
  27.4 7.5 collective-permute-start.31
  35.0 1.9 maximum_reduce_fusion.8
  37.4 2.4 compare_reduce_fusion.8
  44.8 1.7 compare_reduce_fusion.25
  61.0 2.4 collective-permute-start.34
  63.4 4.3 collective-permute-start.1
  67.7 2.9 collective-permute-start.8
  73.2 5.7 copy.23
  79.0 4.2 rev.6
  89.1 4.5 collective-permute-start.29
  95.3 1.9 collective-permute-start.27
  98.4 2.4 collective-permute-start.24
  100.8 3.6 collective-permute-start.32
  114.8 9.1 collective-permute-start.33
  126.5 5.5 collective-permute-start.25
  134.7 4.6 collective-permute-start.5
  139.3 1.9 collective-permute-start.2
  141.2 10.6 collective-permute-start.9
  151.8 2.1 collective-permute-start.26
  189.4 3.0 multiply_convert_fusion.1
  194.7 10.3 copy.26
  205.0 3.9 collective-permute-start.17
  208.9 10.3 collective-permute-start.19
  219.2 1.9 collective-permute-start.22
  221.1 2.4 collective-permute-start.15
  223.5 1.9 collective-permute-start.12
  226.4 3.9 collective-permute-start.20
  235.4 3.9 collective-permute-start.13
  240.9 8.6 collective-permute-start.21
  255.0 2.1 collective-permute-start.14
  315.6 2.9 reshape.552
  318.6 2.6 fusion
  326.5 5.0 fusion.3
  338.7 1.5 concatenate.447
  340.2 1.5 concatenate.448
  341.7 1.5 concatenate.449
  343.8 1.5 concatenate.451
  351.1 1.5 constant_dynamic-update-slice_fusion.26
  352.6 1.5 constant_dynamic-update-slice_fusion.25
  354.1 1.5 constant_dynamic-update-slice_fusion.24
  355.6 1.5 constant_dynamic-update-slice_fusion.23
  357.1 1.5 constant_dynamic-update-slice_fusion.22
  360.0 1.5 constant_dynamic-update-slice_fusion.20
  364.5 1.5 constant_dynamic-update-slice_fusion.17
  369.0 1.5 constant_dynamic-update-slice_fusion.14
  382.1 3.8 copy.29
  386.0 5.4 fusion.61
  392.7 10.6 collective-permute-start.43
  403.3 1.9 collective-permute-start.45
  405.2 1.9 collective-permute-start.46
  407.2 2.4 collective-permute-start.36
  409.6 7.5 collective-permute-start.39
  417.2 3.2 convolution_convert_fusion.1
  420.4 547.1 %all-reduce.8 = (bf16[27,128,128]{2,1,0:T(8,128)(2,1)}, bf16[27,256,256]{2,1,0:T(8,128)(2,1)}) all-reduce(f32[27,128,128]{2,1,0:T(8,128)S(1)} %fusion.3, f32[27,256,256]{2,1,0:T(8,128)} %fusion.61), channel_id=2, replica_groups=mesh['gx'=64,'gy'=4] {'gx'}, use_global_device_ids=true, to_apply=%region_0.9.clone | all-reduce | flops 2211840 | bytes 13271040
  969.0 1.6 dynamic-slice_convert_fusion
  973.1 15.6 %collective-permute-start.37 = (bf16[2,1,1,8,128]{4,3,2,1,0:T(8,128)(2,1)S(1)}, bf16[2,1,1,8,128]{4,3,2,1,0:T(8,128)(2,1)S(1)}, u32[]{:S(2)}, u32[]{:S(2)}) collective-permute-start(bf16[2,1,1,8,128]{4,3,2,1,0:T(8,128)(2,1)S(1)} %collective-permute-done.36), channel_id=1, source_target_pairs={{0,1},{1,2},{2,3},{4,5},{5,6},{6,7},{8,9},{9,10},{10,11},{12,13},{... | collective-permute-start | bytes 12296 | tf_op jit(solution)/shard_map/ppermute | solution.py:18
  992.2 4.5 collective-permute-start.41
  1002.1 1.9 collective-permute-start.38
  1051.4 5.8 convolution_convert_fusion
  1057.1 51.8 %all-reduce.7.cloned.1.call-done = (bf16[27,2,128]{2,1,0:T(2,128)(2,1)}, bf16[8,2,256]{2,0,1:T(8,128)(2,1)}, bf16[27,4,256]{2,1,0:T(4,128)(2,1)}) async-done(((bf16[27,2,128]{2,1,0:T(2,128)(2,1)}, bf16[8,2,256]{2,0,1:T(8,128)(2,1)}, bf16[27,4,256]{2,1,0:T(4,128)(2,1)}), (bf16[27,2,128]{2,1,0:T(2,128)(2,1)}, bf16[8,2,256]{2,0,1:T(8,128)(2,1)}, bf16[27,4,256]{2,1,0:T(4,128)(2,1)})) %all-reduce.7.cloned.1.call-update) | async-done | bytes 77328 | tf_op jit(solution)/shard_map/psum | solution.py:193
  (719 shorter events, 258.3 us)
Async XLA Ops:
  7.2 185.7 %copy-start = (bf16[8,128,256]{2,1,0:T(8,128)(2,1)S(1)}, bf16[8,128,256]{2,1,0:T(8,128)(2,1)}, u32[]{:S(2)}) copy-start(bf16[8,128,256]{2,1,0:T(8,128)(2,1)} %param.26) | copy-start | bytes 1572868
  7.2 1042.8 %reduce-scatter.4.cloned.1.call-start = ((), (), s32[]{:S(2)}) async-start(), calls=%async_computation.1 | async-start | bytes 1064960 | tf_op jit(solution)/shard_map/reduce_scatter | solution.py:189
  7.9 176.8 %copy-start.36 = (pred[2]{0:T(512)(128)(4,1)}, pred[2]{0:T(512)(128)(4,1)S(1)}, u32[]{:S(2)}) copy-start(pred[2]{0:T(512)(128)(4,1)S(1)} %iota_compare_fusion) | copy-start | bytes 10
  9.0 50.6 %collective-permute-start.3 = (bf16[2,1,1,8,128]{4,3,2,1,0:T(8,128)(2,1)S(1)}, bf16[2,1,1,8,128]{4,3,2,1,0:T(8,128)(2,1)S(1)}, u32[]{:S(2)}, u32[]{:S(2)}) collective-permute-start(bf16[2,1,1,8,128]{4,3,2,1,0:T(8,128)(2,1)S(1)} %get-tuple-element.115), channel_id=1, source_target_pairs={{0,4},{4,8},{8,12},{12,16},{16,20},{20,24},{24,28},{28,32},{32,36}... | collective-permute-start | bytes 12296 | tf_op jit(solution)/shard_map/ppermute | solution.py:18
  10.9 50.0 %collective-permute-start = (bf16[2,1,1,8,128]{4,3,2,1,0:T(8,128)(2,1)S(1)}, bf16[2,1,1,8,128]{4,3,2,1,0:T(8,128)(2,1)S(1)}, u32[]{:S(2)}, u32[]{:S(2)}) collective-permute-start(bf16[2,1,1,8,128]{4,3,2,1,0:T(8,128)(2,1)S(1)} %get-tuple-element.116), channel_id=1, source_target_pairs={{0,4},{4,8},{8,12},{12,16},{16,20},{20,24},{24,28},{28,32},{32,36}... | collective-permute-start | bytes 12296 | tf_op jit(solution)/shard_map/ppermute | solution.py:18
  20.1 43.2 %collective-permute-start.7 = (bf16[2,1,1,8,128]{4,3,2,1,0:T(8,128)(2,1)S(1)}, bf16[2,1,1,8,128]{4,3,2,1,0:T(8,128)(2,1)S(1)}, u32[]{:S(2)}, u32[]{:S(2)}) collective-permute-start(bf16[2,1,1,8,128]{4,3,2,1,0:T(8,128)(2,1)S(1)} %get-tuple-element.113), channel_id=1, source_target_pairs={{4,0},{8,4},{12,8},{16,12},{20,16},{24,20},{28,24},{32,28},{36,32}... | collective-permute-start | bytes 12296 | tf_op jit(solution)/shard_map/ppermute | solution.py:18
  23.8 43.8 %collective-permute-start.10 = (bf16[2,1,1,8,128]{4,3,2,1,0:T(8,128)(2,1)S(1)}, bf16[2,1,1,8,128]{4,3,2,1,0:T(8,128)(2,1)S(1)}, u32[]{:S(2)}, u32[]{:S(2)}) collective-permute-start(bf16[2,1,1,8,128]{4,3,2,1,0:T(8,128)(2,1)S(1)} %get-tuple-element.114), channel_id=1, source_target_pairs={{4,0},{8,4},{12,8},{16,12},{20,16},{24,20},{28,24},{32,28},{36,32}... | collective-permute-start | bytes 12296 | tf_op jit(solution)/shard_map/ppermute | solution.py:18
  27.4 71.0 %collective-permute-start.31 = (bf16[2,1,1,4,256]{4,3,2,1,0:T(4,128)(2,1)S(1)}, bf16[2,1,1,4,256]{4,3,2,1,0:T(4,128)(2,1)S(1)}, u32[]{:S(2)}, u32[]{:S(2)}) collective-permute-start(bf16[2,1,1,4,256]{4,3,2,1,0:T(4,128)(2,1)S(1)} %get-tuple-element.149), channel_id=1, source_target_pairs={{4,0},{8,4},{12,8},{16,12},{20,16},{24,20},{28,24},{32,28},{36,32}... | collective-permute-start | bytes 12296 | tf_op jit(solution)/shard_map/ppermute | solution.py:18
  56.9 225.0 %copy-start.38 = (s32[1024]{0:T(1024)}, s32[1024]{0:T(1024)S(1)}, u32[]{:S(2)}) copy-start(s32[1024]{0:T(1024)S(1)} %pad_clamp_fusion.10) | copy-start | bytes 12292
  57.0 220.2 %copy-start.41 = (s32[1024]{0:T(1024)}, s32[1024]{0:T(1024)S(1)}, u32[]{:S(2)}) copy-start(s32[1024]{0:T(1024)S(1)} %pad_clamp_fusion.15) | copy-start | bytes 12292
  57.0 225.6 %copy-start.39 = (s32[1024]{0:T(1024)}, s32[1024]{0:T(1024)S(1)}, u32[]{:S(2)}) copy-start(s32[1024]{0:T(1024)S(1)} %pad_clamp_fusion.9) | copy-start | bytes 12292
  57.0 224.4 %copy-start.40 = (s32[1024]{0:T(1024)}, s32[1024]{0:T(1024)S(1)}, u32[]{:S(2)}) copy-start(s32[1024]{0:T(1024)S(1)} %pad_clamp_fusion.11) | copy-start | bytes 12292
  58.5 224.7 %copy-start.42 = (s32[1024]{0:T(1024)}, s32[1024]{0:T(1024)S(1)}, u32[]{:S(2)}) copy-start(s32[1024]{0:T(1024)S(1)} %pad_clamp_fusion.21) | copy-start | bytes 12292
  58.5 225.9 %copy-start.43 = (s32[1024]{0:T(1024)}, s32[1024]{0:T(1024)S(1)}, u32[]{:S(2)}) copy-start(s32[1024]{0:T(1024)S(1)} %pad_clamp_fusion.20) | copy-start | bytes 12292
  59.6 11.0 collective-permute-start.4
  61.0 39.9 %collective-permute-start.34 = (bf16[2,1,1,4,256]{4,3,2,1,0:T(4,128)(2,1)S(1)}, bf16[2,1,1,4,256]{4,3,2,1,0:T(4,128)(2,1)S(1)}, u32[]{:S(2)}, u32[]{:S(2)}) collective-permute-start(bf16[2,1,1,4,256]{4,3,2,1,0:T(4,128)(2,1)S(1)} %get-tuple-element.150), channel_id=1, source_target_pairs={{4,0},{8,4},{12,8},{16,12},{20,16},{24,20},{28,24},{32,28},{36,32}... | collective-permute-start | bytes 12296 | tf_op jit(solution)/shard_map/ppermute | solution.py:18
  63.4 25.7 %collective-permute-start.1 = (bf16[2,1,1,8,128]{4,3,2,1,0:T(8,128)(2,1)S(1)}, bf16[2,1,1,8,128]{4,3,2,1,0:T(8,128)(2,1)S(1)}, u32[]{:S(2)}, u32[]{:S(2)}) collective-permute-start(bf16[2,1,1,8,128]{4,3,2,1,0:T(8,128)(2,1)S(1)} %collective-permute-done), channel_id=1, source_target_pairs={{0,1},{1,2},{2,3},{4,5},{5,6},{6,7},{8,9},{9,10},{10,11},{12,13},{... | collective-permute-start | bytes 12296 | tf_op jit(solution)/shard_map/ppermute | solution.py:18
  67.7 27.7 %collective-permute-start.8 = (bf16[2,1,1,8,128]{4,3,2,1,0:T(8,128)(2,1)S(1)}, bf16[2,1,1,8,128]{4,3,2,1,0:T(8,128)(2,1)S(1)}, u32[]{:S(2)}, u32[]{:S(2)}) collective-permute-start(bf16[2,1,1,8,128]{4,3,2,1,0:T(8,128)(2,1)S(1)} %collective-permute-done.7), channel_id=1, source_target_pairs={{0,1},{1,2},{2,3},{4,5},{5,6},{6,7},{8,9},{9,10},{10,11},{12,13},{... | collective-permute-start | bytes 12296 | tf_op jit(solution)/shard_map/ppermute | solution.py:18
  70.6 33.9 %collective-permute-start.11 = (bf16[2,1,1,8,128]{4,3,2,1,0:T(8,128)(2,1)S(1)}, bf16[2,1,1,8,128]{4,3,2,1,0:T(8,128)(2,1)S(1)}, u32[]{:S(2)}, u32[]{:S(2)}) collective-permute-start(bf16[2,1,1,8,128]{4,3,2,1,0:T(8,128)(2,1)S(1)} %collective-permute-done.10), channel_id=1, source_target_pairs={{1,0},{2,1},{3,2},{5,4},{6,5},{7,6},{9,8},{10,9},{11,10},{13,12},{... | collective-permute-start | bytes 12296 | tf_op jit(solution)/shard_map/ppermute | solution.py:18
  89.1 50.1 %collective-permute-start.29 = (bf16[2,4,1,4,256]{4,3,2,1,0:T(4,128)(2,1)S(1)}, bf16[2,4,1,4,256]{4,3,2,1,0:T(4,128)(2,1)S(1)}, u32[]{:S(2)}, u32[]{:S(2)}) collective-permute-start(bf16[2,4,1,4,256]{4,3,2,1,0:T(4,128)(2,1)S(1)} %get-tuple-element.155), channel_id=1, source_target_pairs={{0,1},{1,2},{2,3},{4,5},{5,6},{6,7},{8,9},{9,10},{10,11},{12,13},{... | collective-permute-start | bytes 49160 | tf_op jit(solution)/shard_map/ppermute | solution.py:18
  95.3 19.5 %collective-permute-start.27 = (bf16[2,1,1,4,256]{4,3,2,1,0:T(4,128)(2,1)S(1)}, bf16[2,1,1,4,256]{4,3,2,1,0:T(4,128)(2,1)S(1)}, u32[]{:S(2)}, u32[]{:S(2)}) collective-permute-start(bf16[2,1,1,4,256]{4,3,2,1,0:T(4,128)(2,1)S(1)} %get-tuple-element.151), channel_id=1, source_target_pairs={{0,4},{4,8},{8,12},{12,16},{16,20},{20,24},{24,28},{28,32},{32,36}... | collective-permute-start | bytes 12296 | tf_op jit(solution)/shard_map/ppermute | solution.py:18
  98.4 25.5 %collective-permute-start.24 = (bf16[2,1,1,4,256]{4,3,2,1,0:T(4,128)(2,1)S(1)}, bf16[2,1,1,4,256]{4,3,2,1,0:T(4,128)(2,1)S(1)}, u32[]{:S(2)}, u32[]{:S(2)}) collective-permute-start(bf16[2,1,1,4,256]{4,3,2,1,0:T(4,128)(2,1)S(1)} %get-tuple-element.152), channel_id=1, source_target_pairs={{0,4},{4,8},{8,12},{12,16},{16,20},{20,24},{24,28},{28,32},{32,36}... | collective-permute-start | bytes 12296 | tf_op jit(solution)/shard_map/ppermute | solution.py:18
  100.8 24.4 %collective-permute-start.32 = (bf16[2,1,1,4,256]{4,3,2,1,0:T(4,128)(2,1)S(1)}, bf16[2,1,1,4,256]{4,3,2,1,0:T(4,128)(2,1)S(1)}, u32[]{:S(2)}, u32[]{:S(2)}) collective-permute-start(bf16[2,1,1,4,256]{4,3,2,1,0:T(4,128)(2,1)S(1)} %collective-permute-done.31), channel_id=1, source_target_pairs={{0,1},{1,2},{2,3},{4,5},{5,6},{6,7},{8,9},{9,10},{10,11},{12,13},{... | collective-permute-start | bytes 12296 | tf_op jit(solution)/shard_map/ppermute | solution.py:18
  104.5 22.0 %collective-permute-start.35 = (bf16[2,1,1,4,256]{4,3,2,1,0:T(4,128)(2,1)S(1)}, bf16[2,1,1,4,256]{4,3,2,1,0:T(4,128)(2,1)S(1)}, u32[]{:S(2)}, u32[]{:S(2)}) collective-permute-start(bf16[2,1,1,4,256]{4,3,2,1,0:T(4,128)(2,1)S(1)} %collective-permute-done.34), channel_id=1, source_target_pairs={{1,0},{2,1},{3,2},{5,4},{6,5},{7,6},{9,8},{10,9},{11,10},{13,12},{... | collective-permute-start | bytes 12296 | tf_op jit(solution)/shard_map/ppermute | solution.py:18
  114.8 26.4 %collective-permute-start.33 = (bf16[2,1,4,4,256]{4,3,2,1,0:T(4,128)(2,1)S(1)}, bf16[2,1,4,4,256]{4,3,2,1,0:T(4,128)(2,1)S(1)}, u32[]{:S(2)}, u32[]{:S(2)}) collective-permute-start(bf16[2,1,4,4,256]{4,3,2,1,0:T(4,128)(2,1)S(1)} %get-tuple-element.153), channel_id=1, source_target_pairs={{4,0},{8,4},{12,8},{16,12},{20,16},{24,20},{28,24},{32,28},{36,32}... | collective-permute-start | bytes 49160 | tf_op jit(solution)/shard_map/ppermute | solution.py:18
  123.9 27.9 %collective-permute-start.30 = (bf16[2,4,1,4,256]{4,3,2,1,0:T(4,128)(2,1)S(1)}, bf16[2,4,1,4,256]{4,3,2,1,0:T(4,128)(2,1)S(1)}, u32[]{:S(2)}, u32[]{:S(2)}) collective-permute-start(bf16[2,4,1,4,256]{4,3,2,1,0:T(4,128)(2,1)S(1)} %get-tuple-element.156), channel_id=1, source_target_pairs={{1,0},{2,1},{3,2},{5,4},{6,5},{7,6},{9,8},{10,9},{11,10},{13,12},{... | collective-permute-start | bytes 49160 | tf_op jit(solution)/shard_map/ppermute | solution.py:18
  125.2 8.2 collective-permute-start.28
  126.5 8.2 collective-permute-start.25
  133.4 35.1 %collective-permute-start.6 = (bf16[2,8,1,8,128]{4,3,2,1,0:T(8,128)(2,1)S(1)}, bf16[2,8,1,8,128]{4,3,2,1,0:T(8,128)(2,1)S(1)}, u32[]{:S(2)}, u32[]{:S(2)}) collective-permute-start(bf16[2,8,1,8,128]{4,3,2,1,0:T(8,128)(2,1)S(1)} %get-tuple-element.120), channel_id=1, source_target_pairs={{1,0},{2,1},{3,2},{5,4},{6,5},{7,6},{9,8},{10,9},{11,10},{13,12},{... | collective-permute-start | bytes 98312 | tf_op jit(solution)/shard_map/ppermute | solution.py:18
  134.7 35.5 %collective-permute-start.5 = (bf16[2,8,1,8,128]{4,3,2,1,0:T(8,128)(2,1)S(1)}, bf16[2,8,1,8,128]{4,3,2,1,0:T(8,128)(2,1)S(1)}, u32[]{:S(2)}, u32[]{:S(2)}) collective-permute-start(bf16[2,8,1,8,128]{4,3,2,1,0:T(8,128)(2,1)S(1)} %get-tuple-element.119), channel_id=1, source_target_pairs={{0,1},{1,2},{2,3},{4,5},{5,6},{6,7},{8,9},{9,10},{10,11},{12,13},{... | collective-permute-start | bytes 98312 | tf_op jit(solution)/shard_map/ppermute | solution.py:18
  139.3 32.6 %collective-permute-start.2 = (bf16[2,1,8,8,128]{4,3,2,1,0:T(8,128)(2,1)S(1)}, bf16[2,1,8,8,128]{4,3,2,1,0:T(8,128)(2,1)S(1)}, u32[]{:S(2)}, u32[]{:S(2)}) collective-permute-start(bf16[2,1,8,8,128]{4,3,2,1,0:T(8,128)(2,1)S(1)} %get-tuple-element.118), channel_id=1, source_target_pairs={{0,4},{4,8},{8,12},{12,16},{16,20},{20,24},{24,28},{28,32},{32,36}... | collective-permute-start | bytes 98312 | tf_op jit(solution)/shard_map/ppermute | solution.py:18
  141.2 32.4 %collective-permute-start.9 = (bf16[2,1,8,8,128]{4,3,2,1,0:T(8,128)(2,1)S(1)}, bf16[2,1,8,8,128]{4,3,2,1,0:T(8,128)(2,1)S(1)}, u32[]{:S(2)}, u32[]{:S(2)}) collective-permute-start(bf16[2,1,8,8,128]{4,3,2,1,0:T(8,128)(2,1)S(1)} %get-tuple-element.117), channel_id=1, source_target_pairs={{4,0},{8,4},{12,8},{16,12},{20,16},{24,20},{28,24},{32,28},{36,32}... | collective-permute-start | bytes 98312 | tf_op jit(solution)/shard_map/ppermute | solution.py:18
  151.8 15.0 %collective-permute-start.26 = (bf16[2,1,4,4,256]{4,3,2,1,0:T(4,128)(2,1)S(1)}, bf16[2,1,4,4,256]{4,3,2,1,0:T(4,128)(2,1)S(1)}, u32[]{:S(2)}, u32[]{:S(2)}) collective-permute-start(bf16[2,1,4,4,256]{4,3,2,1,0:T(4,128)(2,1)S(1)} %get-tuple-element.154), channel_id=1, source_target_pairs={{0,4},{4,8},{8,12},{12,16},{16,20},{20,24},{24,28},{28,32},{32,36}... | collective-permute-start | bytes 49160 | tf_op jit(solution)/shard_map/ppermute | solution.py:18
  205.0 72.1 %collective-permute-start.17 = (bf16[2,4,1,4,256]{4,3,2,1,0:T(4,128)(2,1)S(1)}, bf16[2,4,1,4,256]{4,3,2,1,0:T(4,128)(2,1)S(1)}, u32[]{:S(2)}, u32[]{:S(2)}) collective-permute-start(bf16[2,4,1,4,256]{4,3,2,1,0:T(4,128)(2,1)S(1)} %get-tuple-element.165), channel_id=1, source_target_pairs={{0,1},{1,2},{2,3},{4,5},{5,6},{6,7},{8,9},{9,10},{10,11},{12,13},{... | collective-permute-start | bytes 49160 | tf_op jit(solution)/shard_map/ppermute | solution.py:18
  208.9 17.5 %collective-permute-start.19 = (bf16[2,1,1,4,256]{4,3,2,1,0:T(4,128)(2,1)S(1)}, bf16[2,1,1,4,256]{4,3,2,1,0:T(4,128)(2,1)S(1)}, u32[]{:S(2)}, u32[]{:S(2)}) collective-permute-start(bf16[2,1,1,4,256]{4,3,2,1,0:T(4,128)(2,1)S(1)} %get-tuple-element.157), channel_id=1, source_target_pairs={{4,0},{8,4},{12,8},{16,12},{20,16},{24,20},{28,24},{32,28},{36,32}... | collective-permute-start | bytes 12296 | tf_op jit(solution)/shard_map/ppermute | solution.py:18
  219.2 11.2 collective-permute-start.22
  221.1 11.8 %collective-permute-start.15 = (bf16[2,1,1,4,256]{4,3,2,1,0:T(4,128)(2,1)S(1)}, bf16[2,1,1,4,256]{4,3,2,1,0:T(4,128)(2,1)S(1)}, u32[]{:S(2)}, u32[]{:S(2)}) collective-permute-start(bf16[2,1,1,4,256]{4,3,2,1,0:T(4,128)(2,1)S(1)} %get-tuple-element.159), channel_id=1, source_target_pairs={{0,4},{4,8},{8,12},{12,16},{16,20},{20,24},{24,28},{28,32},{32,36}... | collective-permute-start | bytes 12296 | tf_op jit(solution)/shard_map/ppermute | solution.py:18
  223.5 11.8 %collective-permute-start.12 = (bf16[2,1,1,4,256]{4,3,2,1,0:T(4,128)(2,1)S(1)}, bf16[2,1,1,4,256]{4,3,2,1,0:T(4,128)(2,1)S(1)}, u32[]{:S(2)}, u32[]{:S(2)}) collective-permute-start(bf16[2,1,1,4,256]{4,3,2,1,0:T(4,128)(2,1)S(1)} %get-tuple-element.160), channel_id=1, source_target_pairs={{0,4},{4,8},{8,12},{12,16},{16,20},{20,24},{24,28},{28,32},{32,36}... | collective-permute-start | bytes 12296 | tf_op jit(solution)/shard_map/ppermute | solution.py:18
  226.4 14.5 %collective-permute-start.20 = (bf16[2,1,1,4,256]{4,3,2,1,0:T(4,128)(2,1)S(1)}, bf16[2,1,1,4,256]{4,3,2,1,0:T(4,128)(2,1)S(1)}, u32[]{:S(2)}, u32[]{:S(2)}) collective-permute-start(bf16[2,1,1,4,256]{4,3,2,1,0:T(4,128)(2,1)S(1)} %collective-permute-done.19), channel_id=1, source_target_pairs={{0,1},{1,2},{2,3},{4,5},{5,6},{6,7},{8,9},{9,10},{10,11},{12,13},{... | collective-permute-start | bytes 12296 | tf_op jit(solution)/shard_map/ppermute | solution.py:18
  230.4 21.2 %collective-permute-start.23 = (bf16[2,1,1,4,256]{4,3,2,1,0:T(4,128)(2,1)S(1)}, bf16[2,1,1,4,256]{4,3,2,1,0:T(4,128)(2,1)S(1)}, u32[]{:S(2)}, u32[]{:S(2)}) collective-permute-start(bf16[2,1,1,4,256]{4,3,2,1,0:T(4,128)(2,1)S(1)} %collective-permute-done.22), channel_id=1, source_target_pairs={{1,0},{2,1},{3,2},{5,4},{6,5},{7,6},{9,8},{10,9},{11,10},{13,12},{... | collective-permute-start | bytes 12296 | tf_op jit(solution)/shard_map/ppermute | solution.py:18
  233.0 22.0 %collective-permute-start.16 = (bf16[2,1,1,4,256]{4,3,2,1,0:T(4,128)(2,1)S(1)}, bf16[2,1,1,4,256]{4,3,2,1,0:T(4,128)(2,1)S(1)}, u32[]{:S(2)}, u32[]{:S(2)}) collective-permute-start(bf16[2,1,1,4,256]{4,3,2,1,0:T(4,128)(2,1)S(1)} %collective-permute-done.15), channel_id=1, source_target_pairs={{1,0},{2,1},{3,2},{5,4},{6,5},{7,6},{9,8},{10,9},{11,10},{13,12},{... | collective-permute-start | bytes 12296 | tf_op jit(solution)/shard_map/ppermute | solution.py:18
  235.4 23.1 %collective-permute-start.13 = (bf16[2,1,1,4,256]{4,3,2,1,0:T(4,128)(2,1)S(1)}, bf16[2,1,1,4,256]{4,3,2,1,0:T(4,128)(2,1)S(1)}, u32[]{:S(2)}, u32[]{:S(2)}) collective-permute-start(bf16[2,1,1,4,256]{4,3,2,1,0:T(4,128)(2,1)S(1)} %collective-permute-done.12), channel_id=1, source_target_pairs={{0,1},{1,2},{2,3},{4,5},{5,6},{6,7},{8,9},{9,10},{10,11},{12,13},{... | collective-permute-start | bytes 12296 | tf_op jit(solution)/shard_map/ppermute | solution.py:18
  240.9 38.3 %collective-permute-start.21 = (bf16[2,1,4,4,256]{4,3,2,1,0:T(4,128)(2,1)S(1)}, bf16[2,1,4,4,256]{4,3,2,1,0:T(4,128)(2,1)S(1)}, u32[]{:S(2)}, u32[]{:S(2)}) collective-permute-start(bf16[2,1,4,4,256]{4,3,2,1,0:T(4,128)(2,1)S(1)} %get-tuple-element.161), channel_id=1, source_target_pairs={{4,0},{8,4},{12,8},{16,12},{20,16},{24,20},{28,24},{32,28},{36,32}... | collective-permute-start | bytes 49160 | tf_op jit(solution)/shard_map/ppermute | solution.py:18
  251.6 29.8 %collective-permute-start.18 = (bf16[2,4,1,4,256]{4,3,2,1,0:T(4,128)(2,1)S(1)}, bf16[2,4,1,4,256]{4,3,2,1,0:T(4,128)(2,1)S(1)}, u32[]{:S(2)}, u32[]{:S(2)}) collective-permute-start(bf16[2,4,1,4,256]{4,3,2,1,0:T(4,128)(2,1)S(1)} %get-tuple-element.166), channel_id=1, source_target_pairs={{1,0},{2,1},{3,2},{5,4},{6,5},{7,6},{9,8},{10,9},{11,10},{13,12},{... | collective-permute-start | bytes 49160 | tf_op jit(solution)/shard_map/ppermute | solution.py:18
  255.0 28.2 %collective-permute-start.14 = (bf16[2,1,4,4,256]{4,3,2,1,0:T(4,128)(2,1)S(1)}, bf16[2,1,4,4,256]{4,3,2,1,0:T(4,128)(2,1)S(1)}, u32[]{:S(2)}, u32[]{:S(2)}) collective-permute-start(bf16[2,1,4,4,256]{4,3,2,1,0:T(4,128)(2,1)S(1)} %get-tuple-element.162), channel_id=1, source_target_pairs={{0,4},{4,8},{8,12},{12,16},{16,20},{20,24},{24,28},{28,32},{32,36}... | collective-permute-start | bytes 49160 | tf_op jit(solution)/shard_map/ppermute | solution.py:18
  392.7 716.3 %all-reduce.7.cloned.1.call-start = ((), (), s32[]{:S(2)}) async-start(), calls=%async_computation.2 | async-start | bytes 154624 | tf_op jit(solution)/shard_map/psum | solution.py:193
  392.7 577.8 %collective-permute-start.43 = (bf16[2,1,1,8,128]{4,3,2,1,0:T(8,128)(2,1)S(1)}, bf16[2,1,1,8,128]{4,3,2,1,0:T(8,128)(2,1)S(1)}, u32[]{:S(2)}, u32[]{:S(2)}) collective-permute-start(bf16[2,1,1,8,128]{4,3,2,1,0:T(8,128)(2,1)S(1)} %copy-done.110), channel_id=1, source_target_pairs={{4,0},{8,4},{12,8},{16,12},{20,16},{24,20},{28,24},{32,28},{36,32}... | collective-permute-start | bytes 12296 | tf_op jit(solution)/shard_map/ppermute | solution.py:18
  403.3 609.4 %collective-permute-start.45 = (bf16[2,1,8,8,128]{4,3,2,1,0:T(8,128)(2,1)S(1)}, bf16[2,1,8,8,128]{4,3,2,1,0:T(8,128)(2,1)S(1)}, u32[]{:S(2)}, u32[]{:S(2)}) collective-permute-start(bf16[2,1,8,8,128]{4,3,2,1,0:T(8,128)(2,1)S(1)} %copy-done.33), channel_id=1, source_target_pairs={{4,0},{8,4},{12,8},{16,12},{20,16},{24,20},{28,24},{32,28},{36,32}... | collective-permute-start | bytes 98312 | tf_op jit(solution)/shard_map/ppermute | solution.py:18
  405.2 566.6 %collective-permute-start.46 = (bf16[2,1,1,8,128]{4,3,2,1,0:T(8,128)(2,1)S(1)}, bf16[2,1,1,8,128]{4,3,2,1,0:T(8,128)(2,1)S(1)}, u32[]{:S(2)}, u32[]{:S(2)}) collective-permute-start(bf16[2,1,1,8,128]{4,3,2,1,0:T(8,128)(2,1)S(1)} %copy-done.109), channel_id=1, source_target_pairs={{4,0},{8,4},{12,8},{16,12},{20,16},{24,20},{28,24},{32,28},{36,32}... | collective-permute-start | bytes 12296 | tf_op jit(solution)/shard_map/ppermute | solution.py:18
  407.2 565.9 %collective-permute-start.36 = (bf16[2,1,1,8,128]{4,3,2,1,0:T(8,128)(2,1)S(1)}, bf16[2,1,1,8,128]{4,3,2,1,0:T(8,128)(2,1)S(1)}, u32[]{:S(2)}, u32[]{:S(2)}) collective-permute-start(bf16[2,1,1,8,128]{4,3,2,1,0:T(8,128)(2,1)S(1)} %copy-done.108), channel_id=1, source_target_pairs={{0,4},{4,8},{8,12},{12,16},{16,20},{20,24},{24,28},{28,32},{32,36}... | collective-permute-start | bytes 12296 | tf_op jit(solution)/shard_map/ppermute | solution.py:18
  409.6 579.2 %collective-permute-start.39 = (bf16[2,1,1,8,128]{4,3,2,1,0:T(8,128)(2,1)S(1)}, bf16[2,1,1,8,128]{4,3,2,1,0:T(8,128)(2,1)S(1)}, u32[]{:S(2)}, u32[]{:S(2)}) collective-permute-start(bf16[2,1,1,8,128]{4,3,2,1,0:T(8,128)(2,1)S(1)} %copy-done.107), channel_id=1, source_target_pairs={{0,4},{4,8},{8,12},{12,16},{16,20},{20,24},{24,28},{28,32},{32,36}... | collective-permute-start | bytes 12296 | tf_op jit(solution)/shard_map/ppermute | solution.py:18
  420.4 547.1 %copy-start.75 = (pred[2]{0:T(512)(128)(4,1)S(1)}, pred[2]{0:T(512)(128)(4,1)}, u32[]{:S(2)}) copy-start(pred[2]{0:T(512)(128)(4,1)} %copy-done.73) | copy-start | bytes 10
  420.4 547.1 %copy-start.78 = (pred[2]{0:T(512)(128)(4,1)S(1)}, pred[2]{0:T(512)(128)(4,1)}, u32[]{:S(2)}) copy-start(pred[2]{0:T(512)(128)(4,1)} %copy-done.76) | copy-start | bytes 10
  420.4 547.1 %copy-start.106 = (pred[2]{0:T(512)(128)(4,1)S(1)}, pred[2]{0:T(512)(128)(4,1)}, u32[]{:S(2)}) copy-start(pred[2]{0:T(512)(128)(4,1)} %copy-done.104) | copy-start | bytes 10
  420.4 571.8 %copy-start.32 = (bf16[2,8,1,8,128]{4,3,2,1,0:T(8,128)(2,1)S(1)}, bf16[2,8,1,8,128]{4,3,2,1,0:T(8,128)(2,1)}, u32[]{:S(2)}) copy-start(bf16[2,8,1,8,128]{4,3,2,1,0:T(8,128)(2,1)} %get-tuple-element.111) | copy-start | bytes 98308
  420.4 578.4 %copy-start.31 = (bf16[2,8,1,8,128]{4,3,2,1,0:T(8,128)(2,1)S(1)}, bf16[2,8,1,8,128]{4,3,2,1,0:T(8,128)(2,1)}, u32[]{:S(2)}) copy-start(bf16[2,8,1,8,128]{4,3,2,1,0:T(8,128)(2,1)} %get-tuple-element.112) | copy-start | bytes 98308
  420.4 581.7 %copy-start.30 = (bf16[2,1,8,8,128]{4,3,2,1,0:T(8,128)(2,1)S(1)}, bf16[2,1,8,8,128]{4,3,2,1,0:T(8,128)(2,1)}, u32[]{:S(2)}) copy-start(bf16[2,1,8,8,128]{4,3,2,1,0:T(8,128)(2,1)} %get-tuple-element.108) | copy-start | bytes 98308
  970.5 21.7 %collective-permute-start.44 = (bf16[2,1,1,8,128]{4,3,2,1,0:T(8,128)(2,1)S(1)}, bf16[2,1,1,8,128]{4,3,2,1,0:T(8,128)(2,1)S(1)}, u32[]{:S(2)}, u32[]{:S(2)}) collective-permute-start(bf16[2,1,1,8,128]{4,3,2,1,0:T(8,128)(2,1)S(1)} %collective-permute-done.43), channel_id=1, source_target_pairs={{0,1},{1,2},{2,3},{4,5},{5,6},{6,7},{8,9},{9,10},{10,11},{12,13},{... | collective-permute-start | bytes 12296 | tf_op jit(solution)/shard_map/ppermute | solution.py:18
  971.8 27.0 %collective-permute-start.47 = (bf16[2,1,1,8,128]{4,3,2,1,0:T(8,128)(2,1)S(1)}, bf16[2,1,1,8,128]{4,3,2,1,0:T(8,128)(2,1)S(1)}, u32[]{:S(2)}, u32[]{:S(2)}) collective-permute-start(bf16[2,1,1,8,128]{4,3,2,1,0:T(8,128)(2,1)S(1)} %collective-permute-done.46), channel_id=1, source_target_pairs={{1,0},{2,1},{3,2},{5,4},{6,5},{7,6},{9,8},{10,9},{11,10},{13,12},{... | collective-permute-start | bytes 12296 | tf_op jit(solution)/shard_map/ppermute | solution.py:18
  973.1 29.0 %collective-permute-start.37 = (bf16[2,1,1,8,128]{4,3,2,1,0:T(8,128)(2,1)S(1)}, bf16[2,1,1,8,128]{4,3,2,1,0:T(8,128)(2,1)S(1)}, u32[]{:S(2)}, u32[]{:S(2)}) collective-permute-start(bf16[2,1,1,8,128]{4,3,2,1,0:T(8,128)(2,1)S(1)} %collective-permute-done.36), channel_id=1, source_target_pairs={{0,1},{1,2},{2,3},{4,5},{5,6},{6,7},{8,9},{9,10},{10,11},{12,13},{... | collective-permute-start | bytes 12296 | tf_op jit(solution)/shard_map/ppermute | solution.py:18
  988.8 16.7 %collective-permute-start.40 = (bf16[2,1,1,8,128]{4,3,2,1,0:T(8,128)(2,1)S(1)}, bf16[2,1,1,8,128]{4,3,2,1,0:T(8,128)(2,1)S(1)}, u32[]{:S(2)}, u32[]{:S(2)}) collective-permute-start(bf16[2,1,1,8,128]{4,3,2,1,0:T(8,128)(2,1)S(1)} %collective-permute-done.39), channel_id=1, source_target_pairs={{1,0},{2,1},{3,2},{5,4},{6,5},{7,6},{9,8},{10,9},{11,10},{13,12},{... | collective-permute-start | bytes 12296 | tf_op jit(solution)/shard_map/ppermute | solution.py:18
  992.2 21.9 %collective-permute-start.41 = (bf16[2,8,1,8,128]{4,3,2,1,0:T(8,128)(2,1)S(1)}, bf16[2,8,1,8,128]{4,3,2,1,0:T(8,128)(2,1)S(1)}, u32[]{:S(2)}, u32[]{:S(2)}) collective-permute-start(bf16[2,8,1,8,128]{4,3,2,1,0:T(8,128)(2,1)S(1)} %copy-done.32), channel_id=1, source_target_pairs={{0,1},{1,2},{2,3},{4,5},{5,6},{6,7},{8,9},{9,10},{10,11},{12,13},{... | collective-permute-start | bytes 98312 | tf_op jit(solution)/shard_map/ppermute | solution.py:18
  998.8 18.1 %collective-permute-start.42 = (bf16[2,8,1,8,128]{4,3,2,1,0:T(8,128)(2,1)S(1)}, bf16[2,8,1,8,128]{4,3,2,1,0:T(8,128)(2,1)S(1)}, u32[]{:S(2)}, u32[]{:S(2)}) collective-permute-start(bf16[2,8,1,8,128]{4,3,2,1,0:T(8,128)(2,1)S(1)} %copy-done.31), channel_id=1, source_target_pairs={{1,0},{2,1},{3,2},{5,4},{6,5},{7,6},{9,8},{10,9},{11,10},{13,12},{... | collective-permute-start | bytes 98312 | tf_op jit(solution)/shard_map/ppermute | solution.py:18
  1002.1 16.8 %collective-permute-start.38 = (bf16[2,1,8,8,128]{4,3,2,1,0:T(8,128)(2,1)S(1)}, bf16[2,1,8,8,128]{4,3,2,1,0:T(8,128)(2,1)S(1)}, u32[]{:S(2)}, u32[]{:S(2)}) collective-permute-start(bf16[2,1,8,8,128]{4,3,2,1,0:T(8,128)(2,1)S(1)} %copy-done.30), channel_id=1, source_target_pairs={{0,4},{4,8},{8,12},{12,16},{16,20},{20,24},{24,28},{28,32},{32,36}... | collective-permute-start | bytes 98312 | tf_op jit(solution)/shard_map/ppermute | solution.py:18
  (98 other events, 5254.9 us)
Sparse Core Ops, SparseCore 0:
  392.8 414.3 reduce-scatter.3
  1051.5 57.4 all-reduce.6
where the time goes:
time: 1120 us
  blocking collectives  547 us (49%)
  local copies, waits for them, and re-layouts  194 us (17%)
  starting transfers between devices  183 us (16%)
  other arithmetic  95.3 us (9%)
  waiting for transfers between devices  54.4 us (5%)
  matrix products  26.9 us (2%)
  between operations  19 us (2%)
    unnamed x1, blocking collectives  547 us
    ppermute x48, starting transfers between devices, shifted(): return lax.ppermute(block, axis, route)  183 us
    unnamed x326, local copies, waits for them, and re-layouts  76.4 us
    gather x104, local copies, waits for them, and re-layouts, surround(): picked = jnp.take(source, jnp.maximum(slot_ids, 0), axis=0)  65.7 us
    select_n x66, other arithmetic, surround(): jnp.where((slot_ids >= 0)[:, None, None, None, None], picked, jnp.zeros((...  57.1 us
    psum x1, waiting for transfers between devices, body(): lax.psum(columns[0].astype(jnp.bfloat16), 'gy').astype(jnp.float32)  51.8 us
  transfers between devices with their start and end apart: 50, of which 3 were waited for; matrix products, arithmetic and copies ran while one was open for 15% of the time, Pallas kernels for 0%

commit v1 on v0

v1 whole, which is shorter than its diff:
```python
import math

import jax
import jax.numpy as jnp
import numpy as np
from jax import lax
from jax.sharding import PartitionSpec as P


def shifted(block, axis, distance):
    devices = range(lax.axis_size(axis))
    route = [(i - distance, i) for i in devices if i - distance in devices]
    return lax.ppermute(block, axis, route)


def send_packed(pieces, axis, distance):
    flat = jnp.concatenate([piece.reshape(-1) for piece in pieces])
    arrived = shifted(flat, axis, distance)
    out, start = [], 0
    for piece in pieces:
        out.append(arrived[start : start + piece.size].reshape(piece.shape))
        start += piece.size
    return out


def extend_xy(fields):
    depth = [f.shape[1] for f in fields]
    from_left = send_packed([f[:, e - 1 : e] for f, e in zip(fields, depth)], "gx", 1)
    from_right = send_packed([f[:, 0:1] for f in fields], "gx", -1)
    wide = [jnp.concatenate([l, f, r], axis=1) for l, f, r in zip(from_left, fields, from_right)]
    from_down = send_packed([w[:, :, e - 1 : e] for w, e in zip(wide, depth)], "gy", 1)
    from_up = send_packed([w[:, :, 0:1] for w in wide], "gy", -1)
    return [jnp.concatenate([d, w, u], axis=2) for d, w, u in zip(from_down, wide, from_up)]


def source_table(slot_table, extent):
    slot_count = slot_table.shape[0]
    own = jnp.arange(slot_count, dtype=slot_table.dtype)[:, None]
    full = jnp.concatenate([slot_table[:, :13], own, slot_table[:, 13:]], axis=1)
    full = full.reshape(slot_count, 3, 3, 3)
    reps = np.array([1, extent, 1])
    for axis in (1, 2, 3):
        full = jnp.repeat(full, reps, axis=axis, total_repeat_length=extent + 2)
    return full


def pad_field(wide, sources):
    extent = wide.shape[3]
    tall = jnp.concatenate([wide[:, :, :, extent - 1 :], wide, wide[:, :, :, :1]], axis=3)
    padded = jnp.zeros((sources.shape[0],) + tall.shape[1:], tall.dtype)
    for slot in range(tall.shape[0]):
        padded = jnp.where((sources == slot)[..., None], tall[slot][None], padded)
    return padded


def unfold(padded, extent):
    windows = []
    for along_x in range(3):
        for along_y in range(3):
            for along_z in range(3):
                windows.append(
                    padded[
                        :,
                        along_x : along_x + extent,
                        along_y : along_y + extent,
                        along_z : along_z + extent,
                        :,
                    ]
                )
    stacked = jnp.concatenate(windows, axis=-1)
    return stacked.reshape(-1, stacked.shape[-1])


def into_cells(blocks, half_edge):
    slot_count, channels = (blocks.shape[0], blocks.shape[-1])
    lattice = blocks.reshape(slot_count, half_edge, 2, half_edge, 2, half_edge, 2, channels)
    lattice = lattice.transpose(0, 1, 3, 5, 2, 4, 6, 7)
    return lattice.reshape(slot_count * half_edge**3, 8 * channels)


def from_cells(cell_rows, slot_count, half_edge, channels):
    lattice = cell_rows.reshape(slot_count, half_edge, half_edge, half_edge, 2, 2, 2, channels)
    lattice = lattice.transpose(0, 1, 4, 2, 5, 3, 6, 7)
    return lattice.reshape(slot_count, 2 * half_edge, 2 * half_edge, 2 * half_edge, channels)


def silu_slope(values):
    logistic = jax.nn.sigmoid(values)
    return logistic * (1.0 + values * (1.0 - logistic))


def contract_rows(left, right):
    return lax.dot_general(
        left, right, (((0,), (0,)), ((), ())), preferred_element_type=jnp.float32
    )


def reduce_terms(terms):
    blocks = lax.axis_size("gx")
    quarters = lax.axis_size("gy")
    rows = [t.transpose(1, 0, 2).reshape(blocks, -1) for t in terms]
    packed = jnp.concatenate(rows, axis=1)
    width = packed.shape[1]
    packed = packed.reshape(blocks, quarters, width // quarters).transpose(1, 0, 2)
    part = lax.psum_scatter(packed.astype(jnp.bfloat16), "gy", scatter_dimension=0, tiled=True)
    part = part[0].astype(jnp.float32).reshape(blocks * 8, -1)
    part = lax.psum_scatter(part, "gx", scatter_dimension=0, tiled=True)
    row = lax.all_gather(part, "gy", axis=0, tiled=True).reshape(-1)
    out, start = [], 0
    for t in terms:
        size = t.size // blocks
        piece = row[start : start + size].reshape(t.shape[1] // blocks, t.shape[0], t.shape[2])
        out.append(piece.transpose(1, 0, 2))
        start += size
    return out


def body(features, cotangent, conv_first, down_weight, conv_second, block_count, neighbours):
    inputs = features[0, 0]
    slot_count, extent, channels = (inputs.shape[0], inputs.shape[1], inputs.shape[-1])
    half_edge = extent // 2
    wide_channels = conv_second.shape[-1]
    slot_table = neighbours[0, 0]
    live_mask = (jnp.arange(slot_count) < block_count[0, 0])[:, None, None, None, None]
    inputs = jnp.where(live_mask, inputs, jnp.zeros((), inputs.dtype))
    seed_blocks = jnp.where(live_mask, cotangent[0, 0], jnp.zeros((), inputs.dtype))
    sources_full = source_table(slot_table, extent)
    sources_half = source_table(slot_table, half_edge)

    wide_input, wide_seed = extend_xy([inputs, seed_blocks])
    first_cols = unfold(pad_field(wide_input, sources_full), extent)
    first_matrix = conv_first.reshape(-1, channels)
    pre_first = jnp.dot(first_cols, first_matrix, preferred_element_type=jnp.float32)
    hidden_first = jax.nn.silu(pre_first).astype(jnp.bfloat16)
    first_cells = into_cells(
        hidden_first.reshape(slot_count, extent, extent, extent, channels), half_edge
    )
    down_matrix = down_weight.reshape(-1, wide_channels)
    pre_down = jnp.dot(first_cells, down_matrix, preferred_element_type=jnp.float32)
    hidden_down = (
        jax.nn.silu(pre_down)
        .astype(jnp.bfloat16)
        .reshape(slot_count, half_edge, half_edge, half_edge, wide_channels)
    )
    (wide_hidden,) = extend_xy([hidden_down])
    second_cols = unfold(pad_field(wide_hidden, sources_half), half_edge)
    second_matrix = conv_second.reshape(-1, wide_channels)
    output_field = jnp.dot(second_cols, second_matrix, preferred_element_type=jnp.float32).astype(
        jnp.bfloat16
    )
    seed_cols = unfold(pad_field(wide_seed, sources_half), half_edge)
    second_flip = jnp.transpose(conv_second[::-1], (0, 2, 1)).reshape(-1, wide_channels)
    back_down = jnp.dot(seed_cols, second_flip, preferred_element_type=jnp.float32)
    delta_down = (back_down * silu_slope(pre_down)).astype(jnp.bfloat16)
    grad_second = contract_rows(second_cols, seed_blocks.reshape(-1, wide_channels))
    grad_down = contract_rows(first_cells, delta_down)
    second_sum, down_sum = reduce_terms(
        [
            grad_second.reshape(27, wide_channels, wide_channels),
            grad_down.reshape(8, channels, wide_channels),
        ]
    )
    back_cells = lax.dot_general(
        delta_down, down_matrix, (((1,), (1,)), ((), ())), preferred_element_type=jnp.float32
    )
    back_first = from_cells(back_cells, slot_count, half_edge, channels).reshape(-1, channels)
    delta_first = (back_first * silu_slope(pre_first)).astype(jnp.bfloat16)
    delta_blocks = delta_first.reshape(slot_count, extent, extent, extent, channels)
    (wide_delta,) = extend_xy([delta_blocks])
    delta_cols = unfold(pad_field(wide_delta, sources_full), extent)
    first_flip = jnp.transpose(conv_first[::-1], (0, 2, 1)).reshape(-1, channels)
    input_grad = jnp.dot(delta_cols, first_flip, preferred_element_type=jnp.float32).astype(
        jnp.bfloat16
    )
    grad_first = contract_rows(first_cols, delta_first)
    (first_sum,) = reduce_terms([grad_first.reshape(27, channels, channels)])
    devices = lax.axis_size("gx") * lax.axis_size("gy")
    scale_first = 1.0 / math.sqrt(float(devices * slot_count * extent**3))
    scale_half = 1.0 / math.sqrt(float(devices * slot_count * half_edge**3))
    return (
        output_field.reshape(1, 1, slot_count, half_edge, half_edge, half_edge, wide_channels),
        input_grad.reshape(1, 1, slot_count, extent, extent, extent, channels),
        first_sum * scale_first,
        down_sum * scale_half,
        second_sum * scale_half,
    )


def solution(mesh):
    placed = (
        P("gx", "gy", None, None, None, None, None),
        P("gx", "gy", None, None, None, None, None),
        P(),
        P(),
        P(),
        P("gx", "gy"),
        P("gx", "gy", None, None),
    )
    return jax.shard_map(
        body,
        mesh=mesh,
        in_specs=placed,
        out_specs=(
            P("gx", "gy", None, None, None, None, None),
            P("gx", "gy", None, None, None, None, None),
            P(None, "gx", None),
            P(None, "gx", None),
            P(None, "gx", None),
        ),
        check_vma=False,
    )
```

time: 1120 us -> 1130 us (level)
  the two profiles are of different devices: /device:TPU:2 before, /device:TPU:0 now
where the time goes in v1:
time: 1130 us
  waiting for transfers between devices  886 us (78%)
  local copies, waits for them, and re-layouts  129 us (11%)
  starting transfers between devices  37.5 us (3%)
  blocking collectives  26.8 us (2%)
  matrix products  22 us (2%)
  between operations  15.5 us (1%)
    reduce_scatter x2, waiting for transfers between devices, reduce_terms(): part = lax.psum_scatter(part, 'gx', scatter_dimension=0, tiled=True)  797 us
    reduce_scatter x2, waiting for transfers between devices, reduce_terms(): lax.psum_scatter(packed.astype(jnp.bfloat16), 'gy', scatter_dimension=0,...  79.3 us
    unnamed x135, local copies, waits for them, and re-layouts  69.9 us
    ppermute x12, starting transfers between devices, shifted(): return lax.ppermute(block, axis, route)  37.3 us
    all_gather x2, blocking collectives, reduce_terms(): row = lax.all_gather(part, 'gy', axis=0, tiled=True).reshape(-1)  26.8 us
  transfers between devices with their start and end apart: 16, of which 7 were waited for; matrix products, arithmetic and copies ran while one was open for 7% of the time, Pallas kernels for 0%

profile of v1, /device:TPU:0, one launch (start us, length us, event | category | flops | bytes accessed | tf_op | source)
XLA Modules:
  0.0 1126.4 jit_solution(13630961306361791147)
XLA Ops:
  7.9 0.9 bitcast_select_fusion.1
  8.9 1.0 bitcast_select_fusion
  10.0 1.3 collective-permute-start
  11.3 1.3 collective-permute-start.1
  12.6 0.8 fusion.17
  18.8 1.4 collective-permute-done.1
  20.4 2.9 collective-permute-start.2
  23.3 1.3 collective-permute-start.3
  25.5 5.7 copy.82
  31.3 4.1 rev.6
  36.7 1.2 select_select_fusion.1
  41.5 2.0 multiply_convert_fusion.1
  44.5 0.9 multiply_convert_fusion.2
  45.5 8.3 collective-permute-start.4
  53.8 1.3 collective-permute-start.5
  55.8 5.3 collective-permute-done.5
  61.2 4.5 collective-permute-start.6
  65.8 1.5 collective-permute-start.7
  67.5 10.3 copy.85
  96.7 2.9 reshape.459
  99.6 2.6 fusion.2
  102.8 1.1 reshape.474
  122.0 2.9 reshape.454
  125.0 2.3 copy.88
  127.2 2.5 convert_bitcast_fusion
  129.8 4.2 copy.89
  133.9 5.5 reshape.473
  140.2 5.0 fusion
  145.8 2.1 convert_element_type.59
  147.9 2.3 copy.87
  150.3 2.3 pad_maximum_fusion
  152.5 2.3 copy.110
  154.9 8.0 collective-permute-start.8
  163.0 1.3 collective-permute-start.9
  164.3 1.9 copy.84
  166.2 1.0 rev.7
  167.2 4.3 collective-permute-start.10
  171.5 1.3 collective-permute-start.11
  172.8 2.6 convolution_convert_fusion.3
  176.1 2.8 collective-permute-done.11
  179.4 1.2 select_select_fusion
  181.5 0.8 slice_dynamic-update-slice_fusion.25
  182.3 0.8 slice_dynamic-update-slice_fusion.24
  183.1 0.8 slice_dynamic-update-slice_fusion.23
  183.9 0.8 slice_dynamic-update-slice_fusion.22
  185.6 0.8 slice_dynamic-update-slice_fusion.20
  186.4 0.8 slice_dynamic-update-slice_fusion.19
  188.0 2.9 reduce-scatter.5.cloned.1.call-done
  190.9 2.1 reshape.476
  193.9 0.9 slice_dynamic-update-slice_fusion.16
  194.8 0.8 slice_dynamic-update-slice_fusion.15
  196.4 76.4 %reduce-scatter.9.cloned.1.call-done = bf16[1,64,7936]{2,1,0:T(8,128)(2,1)} async-done(((bf16[4,64,7936]{2,1,0:T(8,128)(2,1)}), bf16[1,64,7936]{2,1,0:T(8,128)(2,1)}) %reduce-scatter.9.cloned.1.call-update) | async-done | bytes 1015824 | tf_op jit(solution)/shard_map/reduce_scatter | solution.py:105
  272.8 3.7 reshape.477
  278.9 0.9 slice_dynamic-update-slice_fusion.10
  279.8 0.8 slice_dynamic-update-slice_fusion.9
  281.4 0.8 slice_dynamic-update-slice_fusion.7
  283.9 0.8 slice_dynamic-update-slice_fusion.4
  284.7 0.8 slice_dynamic-update-slice_fusion.3
  286.3 0.8 slice_dynamic-update-slice_fusion.1
  288.0 5.8 convolution_convert_fusion.2
  293.7 398.2 %reduce-scatter.7.cloned.1.call-done = f32[8,216]{1,0:T(8,128)} async-done(((f32[512,216]{1,0:T(8,128)}), f32[8,216]{1,0:T(8,128)}) %reduce-scatter.7.cloned.1.call-update) | async-done | bytes 6928 | tf_op jit(solution)/shard_map/reduce_scatter | solution.py:107
  691.9 13.3 %all_gather.6 = f32[32,216]{1,0:T(8,128)S(1)} all-gather(f32[8,216]{1,0:T(8,128)} %reduce-scatter.7.cloned.1.call-done), channel_id=1, replica_groups=mesh['gx'=64,'gy'=4] {'gy'}, dimensions={0}, use_global_device_ids=true | all-gather | bytes 34560 | tf_op jit(solution)/shard_map/all_gather | solution.py:108
  705.9 398.8 %reduce-scatter.11.cloned.1.call-done = f32[8,992]{1,0:T(8,128)} async-done(((f32[512,992]{1,0:T(8,128)}), f32[8,992]{1,0:T(8,128)}) %reduce-scatter.11.cloned.1.call-update) | async-done | bytes 31760 | tf_op jit(solution)/shard_map/reduce_scatter | solution.py:107
  1104.7 13.5 %all_gather.7 = f32[32,992]{1,0:T(8,128)S(1)} all-gather(f32[8,992]{1,0:T(8,128)} %reduce-scatter.11.cloned.1.call-done), channel_id=1, replica_groups=mesh['gx'=64,'gy'=4] {'gy'}, dimensions={0}, use_global_device_ids=true | all-gather | bytes 158720 | tf_op jit(solution)/shard_map/all_gather | solution.py:108
  (225 shorter events, 66.1 us)
Async XLA Ops:
  7.2 37.4 %copy-start = (bf16[8,128,256]{2,1,0:T(8,128)(2,1)S(1)}, bf16[8,128,256]{2,1,0:T(8,128)(2,1)}, u32[]{:S(2)}) copy-start(bf16[8,128,256]{2,1,0:T(8,128)(2,1)} %param.24) | copy-start | bytes 1572868
  7.2 9.4 copy-start.7
  7.2 183.7 %reduce-scatter.5.cloned.1.call-start = ((), (), s32[]{:S(2)}) async-start(), calls=%async_computation.4 | async-start | bytes 1146880 | tf_op jit(solution)/shard_map/reduce_scatter | solution.py:105
  10.0 8.7 collective-permute-start
  11.3 8.8 collective-permute-start.1
  20.4 15.7 %collective-permute-start.2 = (bf16[32768]{0:T(1024)(128)(2,1)S(1)}, bf16[32768]{0:T(1024)(128)(2,1)S(1)}, u32[]{:S(2)}, u32[]{:S(2)}) collective-permute-start(bf16[32768]{0:T(1024)(128)(2,1)S(1)} %pad_maximum_fusion.21), channel_id=1, source_target_pairs={{0,1},{1,2},{2,3},{4,5},{5,6},{6,7},{8,9},{9,10},{10,11},{12,13},{... | collective-permute-start | bytes 196616 | tf_op jit(solution)/shard_map/ppermute | solution.py:13
  23.3 12.7 %collective-permute-start.3 = (bf16[32768]{0:T(1024)(128)(2,1)S(1)}, bf16[32768]{0:T(1024)(128)(2,1)S(1)}, u32[]{:S(2)}, u32[]{:S(2)}) collective-permute-start(bf16[32768]{0:T(1024)(128)(2,1)S(1)} %pad_maximum_fusion.22), channel_id=1, source_target_pairs={{1,0},{2,1},{3,2},{5,4},{6,5},{7,6},{9,8},{10,9},{11,10},{13,12},{... | collective-permute-start | bytes 196616 | tf_op jit(solution)/shard_map/ppermute | solution.py:13
  40.3 1.2 copy-start.4
  41.2 2.9 copy-start.2
  45.5 10.2 collective-permute-start.4
  53.8 7.3 collective-permute-start.5
  61.2 16.5 %collective-permute-start.6 = (bf16[12288]{0:T(1024)(128)(2,1)S(1)}, bf16[12288]{0:T(1024)(128)(2,1)S(1)}, u32[]{:S(2)}, u32[]{:S(2)}) collective-permute-start(bf16[12288]{0:T(1024)(128)(2,1)S(1)} %bitcast.201), channel_id=1, source_target_pairs={{0,1},{1,2},{2,3},{4,5},{5,6},{6,7},{8,9},{9,10},{10,11},{12,13},{... | collective-permute-start | bytes 73736 | tf_op jit(solution)/shard_map/ppermute | solution.py:13
  65.8 12.0 %collective-permute-start.7 = (bf16[12288]{0:T(1024)(128)(2,1)S(1)}, bf16[12288]{0:T(1024)(128)(2,1)S(1)}, u32[]{:S(2)}, u32[]{:S(2)}) collective-permute-start(bf16[12288]{0:T(1024)(128)(2,1)S(1)} %bitcast.202), channel_id=1, source_target_pairs={{1,0},{2,1},{3,2},{5,4},{6,5},{7,6},{9,8},{10,9},{11,10},{13,12},{... | collective-permute-start | bytes 73736 | tf_op jit(solution)/shard_map/ppermute | solution.py:13
  124.9 2.3 copy-start.6
  147.9 2.3 copy-start.3
  150.2 122.6 %reduce-scatter.9.cloned.1.call-start = ((), (), s32[]{:S(2)}) async-start(), calls=%async_computation.6 | async-start | bytes 5079040 | tf_op jit(solution)/shard_map/reduce_scatter | solution.py:105
  154.9 537.0 %reduce-scatter.7.cloned.1.call-start = ((), (), s32[]{:S(2)}) async-start(), calls=%async_computation.5 | async-start | bytes 532480 | tf_op jit(solution)/shard_map/reduce_scatter | solution.py:107
  154.9 12.3 %collective-permute-start.8 = (bf16[16384]{0:T(1024)(128)(2,1)S(1)}, bf16[16384]{0:T(1024)(128)(2,1)S(1)}, u32[]{:S(2)}, u32[]{:S(2)}) collective-permute-start(bf16[16384]{0:T(1024)(128)(2,1)S(1)} %bitcast.200), channel_id=1, source_target_pairs={{0,4},{4,8},{8,12},{12,16},{16,20},{20,24},{24,28},{28,32},{32,36}... | collective-permute-start | bytes 98312 | tf_op jit(solution)/shard_map/ppermute | solution.py:13
  163.0 4.2 collective-permute-start.9
  167.2 8.9 collective-permute-start.10
  171.5 7.3 collective-permute-start.11
  193.0 911.7 %reduce-scatter.11.cloned.1.call-start = ((), (), s32[]{:S(2)}) async-start(), calls=%async_computation.7 | async-start | bytes 2129920 | tf_op jit(solution)/shard_map/reduce_scatter | solution.py:107
  282.3 5.7 copy-start.5
  287.9 831.9 %copy-start.1 = (bf16[8,128,256]{2,1,0:T(8,128)(2,1)S(1)}, bf16[8,128,256]{2,1,0:T(8,128)(2,1)}, u32[]{:S(2)}) copy-start(bf16[8,128,256]{2,1,0:T(8,128)(2,1)} %param.24) | copy-start | bytes 1572868
Sparse Core Ops, SparseCore 0:
  150.3 40.5 reduce-scatter.4
  193.5 79.3 reduce-scatter.8
  275.3 416.5 reduce-scatter.6
  694.2 410.4 reduce-scatter.10
